TPU v7x, 256 devices: a whole 4x4x8 slice. The times are simulated.
256 devices in a mesh: member: 8 (over x, y_hi), space: 32 (over y_lo, z, core).
Axes of the slice: x: 4, y: 4 (y_hi: 2, y_lo: 2; y = y_hi * 2 + y_lo), z: 8, core: 2. Of those that a mesh axis runs over, the one named last changes fastest.
Arguments:
- ensemble: bfloat16 [256, 48, 16384], P('member', None, 'space')
- inflation: float32 [256, 128], P('member'), may hold values from 0.5 to 2
- weights: bfloat16 [128, 256, 256], P('space')
- region_ids: int32 [16384], P('space'), may hold values from 0 to 127, as said below
- extinction: float32 [48], replicated, may hold values from 0.1 to 2
- obs_cols: int32 [4096], P('space'), may hold values from 0 to 16383, as said below
Outputs:
- analysis: bfloat16 [256, 48, 16384], P('member', None, 'space')
- obs_analysis: float32 [256, 4096], P('member', 'space')
Inputs may be any that keep to these rules, and one draw needn't show every extreme that they name: `region_ids`: region r belongs to index r // 4 of space. Each block of 512 columns held by one index of space holds exactly 16 columns of the regions of every index of space. `obs_cols`: each observation's column lies in the block of 512 columns held by the same index of space as the observation.
All inputs are finite; a program needn't handle non-finite values.
Results may differ from a plain program's by a relative error of at most 0.0047.
Values may be sent and summed in bfloat16 or wider, within the bound.
No kernel may reach another device: no remote copies, remote signals or barrier semaphores. Data moves between devices by JAX's collectives and lax.ppermute only.
A program may use at most 64 MiB of HBM per device.

v0:
```python
import jax
import jax.numpy as jnp
from jax import lax
from jax.sharding import PartitionSpec as P


def local(ensemble, inflation, weights, region_ids, extinction, obs_cols):
    n_space = lax.axis_size("space")
    n_member = lax.axis_size("member")
    local_members = ensemble.shape[0]
    tracers = ensemble.shape[1]
    columns = ensemble.shape[2]
    members = local_members * n_member
    reg_count = weights.shape[0]
    all_regions = inflation.shape[1]
    send_cols = columns // n_space
    slot_cols = send_cols // n_member
    own_cols = n_space * slot_cols
    owner = region_ids // reg_count
    owner_hot = (owner[:, None] == jnp.arange(n_space, dtype=jnp.int32)[None, :]).astype(jnp.int32)
    before = jnp.cumsum(owner_hot, axis=0) - owner_hot
    rank_in = jnp.sum(before * owner_hot, axis=1)
    position = owner * send_cols + rank_in
    ordering = (
        jnp.zeros((columns,), jnp.int32).at[position].set(jnp.arange(columns, dtype=jnp.int32))
    )
    labels_all = jnp.take(region_ids % reg_count, ordering).reshape(n_space, n_member, slot_cols)
    my_labels = lax.dynamic_index_in_dim(labels_all, lax.axis_index("member"), 1, keepdims=False)
    got_labels = lax.all_to_all(
        my_labels, "space", split_axis=0, concat_axis=0, tiled=True
    ).reshape(own_cols)
    summed = lax.psum(jnp.sum(ensemble, axis=0, dtype=jnp.float32), "member")
    mean = summed / members
    region_hot = (jnp.arange(all_regions, dtype=jnp.int32)[:, None] == region_ids[None, :]).astype(
        jnp.float32
    )
    factor = jnp.dot(inflation, region_hot, precision=lax.Precision.HIGHEST)
    outgoing = ((ensemble.astype(jnp.float32) - mean[None]) * factor[:, None, :]).astype(
        jnp.bfloat16
    )
    rows_major = jnp.transpose(outgoing, (2, 0, 1)).reshape(columns, local_members * tracers)
    payload = jnp.take(rows_major, ordering, axis=0).reshape(
        n_space, n_member, slot_cols, local_members * tracers
    )
    received = lax.all_to_all(
        lax.all_to_all(payload, "member", split_axis=1, concat_axis=3, tiled=True),
        "space",
        split_axis=0,
        concat_axis=0,
        tiled=True,
    )
    gathered = received.reshape(own_cols, members, tracers)
    accum = jnp.zeros((own_cols, members, tracers), jnp.float32)
    for region in range(reg_count):
        partial_prod = jnp.einsum(
            "jk,cjt->ckt", weights[region], gathered, preferred_element_type=jnp.float32
        )
        accum = accum + jnp.where((got_labels == region)[:, None, None], partial_prod, 0.0)
    increment = accum.astype(jnp.bfloat16)
    result_rows = increment
    result_rows = result_rows.reshape(n_space, 1, slot_cols, members * tracers)
    halfway = lax.all_to_all(result_rows, "space", split_axis=0, concat_axis=0, tiled=True)
    returned = lax.all_to_all(halfway, "member", split_axis=3, concat_axis=1, tiled=True)
    restored = jnp.take(returned.reshape(columns, local_members * tracers), position, axis=0)
    restored = jnp.transpose(restored.reshape(columns, local_members, tracers), (1, 2, 0))
    analysis = (mean[None] + restored.astype(jnp.float32)).astype(jnp.bfloat16)
    local_index = obs_cols - lax.axis_index("space") * columns
    picked = jnp.take(analysis, local_index, axis=2).astype(jnp.float32)
    obs_analysis = jnp.einsum("t,kto->ko", extinction, picked, precision=lax.Precision.HIGHEST)
    return (analysis, obs_analysis)


def solution(mesh):
    in_specs = (
        P("member", None, "space"),
        P("member", None),
        P("space", None, None),
        P("space"),
        P(),
        P("space"),
    )
    out_specs = (P("member", None, "space"), P("member", "space"))
    return jax.shard_map(local, mesh=mesh, in_specs=in_specs, out_specs=out_specs, check_vma=False)
```

profile of v0, /device:TPU:64, one launch (start us, length us, event | category | flops | bytes accessed | tf_op | source)
XLA Modules:
  0.0 389.3 jit_solution(15727001249137828852)
XLA Ops:
  7.2 7.2 %copy.60 = bf16[32,48,512]{1,0,2:T(8,128)(2,1)} copy(bf16[32,48,512]{2,1,0:T(8,128)(2,1)} %param.8) | data formatting | bytes 3145728 | tf_op args[0]
  14.5 4.8 %convert_reduce_fusion = f32[48,512]{0,1:T(8,128)} fusion(bf16[32,48,512]{1,0,2:T(8,128)(2,1)} %copy.60), kind=kLoop, calls=%fused_computation.6 | loop fusion | flops 1548288 | bytes 1671168 | tf_op jit(solution)/shard_map/reduce_sum | solution.py:32
  23.6 3.5 gather_fusion
  27.2 83.8 %all-reduce.2.cloned.1.call-done = f32[48,512]{0,1:T(8,128)} async-done(((f32[48,512]{0,1:T(8,128)}), f32[48,512]{0,1:T(8,128)}) %all-reduce.2.cloned.1.call-update) | async-done | bytes 98320 | tf_op jit(solution)/shard_map/psum | solution.py:32
  112.0 5.8 %fusion.3 = bf16[512,32,48]{2,1,0:T(8,128)(2,1)} fusion(bf16[32,48,512]{1,0,2:T(8,128)(2,1)} %copy.60, f32[32,512]{0,1:T(8,128)S(1)} %copy.62, f32[48,512]{0,1:T(8,128)S(1)} %broadcast_multiply_fusion), kind=kLoop, calls=%fused_computation.11 | loop fusion | flops 3145728 | bytes 3309568 | tf_op jit(solution)/shard_map/transpose | solution.py:41
  117.8 4.4 %copy.63 = bf16[512,32,48]{0,2,1:T(8,128)(2,1)S(1)} copy(bf16[512,32,48]{2,1,0:T(8,128)(2,1)} %fusion.3) | data formatting | bytes 3145728 | tf_op jit(solution)/shard_map/transpose | solution.py:41
  130.6 3.6 all-to-all-start.1
  134.9 16.7 %all-to-all-done.1 = bf16[32,8,2,1536]{3,2,0,1:T(2,128)(2,1)S(1)} async-done(((bf16[32,8,2,1536]{3,2,0,1:T(2,128)(2,1)}), bf16[32,8,2,1536]{3,2,0,1:T(2,128)(2,1)S(1)}, u32[]{:S(2)}, u32[]{:S(2)}) %all-to-all-start.1) | async-done | bytes 1572896 | tf_op jit(solution)/shard_map/all_to_all | solution.py:46
  151.6 8.0 %all-to-all-start = ((s32[32,1,2]{2,1,0:T(1,128)}), s32[32,1,2]{2,1,0:T(1,128)S(1)}, u32[]{:S(2)}, u32[]{:S(2)}) async-start(s32[32,1,2]{2,1,0:T(1,128)} %constant_dynamic-slice_fusion), calls=%async_computation | async-start | bytes 32768 | tf_op jit(solution)/shard_map/all_to_all | solution.py:29
  165.8 6.0 %all-to-all-start.2 = ((bf16[32,1,2,12288]{3,2,1,0:T(2,128)(2,1)}), bf16[32,1,2,12288]{3,2,1,0:T(2,128)(2,1)S(1)}, u32[]{:S(2)}, u32[]{:S(2)}) async-start(bf16[32,1,2,12288]{3,2,1,0:T(2,128)(2,1)} %reshape.160), calls=%async_computation.2 | async-start | bytes 3145728 | tf_op jit(solution)/shard_map/all_to_all | solution.py:45
  172.5 37.2 %all-to-all-done.2 = bf16[32,1,2,12288]{3,2,1,0:T(2,128)(2,1)S(1)} async-done(((bf16[32,1,2,12288]{3,2,1,0:T(2,128)(2,1)}), bf16[32,1,2,12288]{3,2,1,0:T(2,128)(2,1)S(1)}, u32[]{:S(2)}, u32[]{:S(2)}) %all-to-all-start.2) | async-done | bytes 1572896 | tf_op jit(solution)/shard_map/all_to_all | solution.py:45
  209.6 5.2 %reshape.101 = bf16[64,256,48]{2,1,0:T(8,128)(2,1)} reshape(bf16[32,1,2,12288]{3,2,1,0:T(2,128)(2,1)S(1)} %all-to-all-done.2) | data formatting | bytes 3145728 | tf_op jit(solution)/shard_map/reshape | solution.py:52
  214.8 3.6 fusion.10
  226.4 9.3 %reshape.102 = bf16[32,1,2,12288]{3,2,0,1:T(2,128)(2,1)S(1)} reshape(bf16[64,256,48]{2,1,0:T(8,128)(2,1)} %copy.72) | data formatting | bytes 3145728 | tf_op jit(solution)/shard_map/reshape | solution.py:61
  235.7 44.2 %all_to_all.49 = bf16[32,1,2,12288]{3,2,1,0:T(2,128)(2,1)S(1)} all-to-all(bf16[32,1,2,12288]{3,2,1,0:T(2,128)(2,1)S(1)} %bitcast.79), channel_id=1, replica_groups=mesh['member'=8,'space'=32] {'space'}, dimensions={0} | all-to-all | bytes 3145728 | tf_op jit(solution)/shard_map/all_to_all | solution.py:62
  280.0 11.1 %copy.74 = bf16[32,1,2,12288]{0,2,1,3:T(2,128)(2,1)} copy(bf16[32,1,2,12288]{3,2,1,0:T(2,128)(2,1)S(1)} %all_to_all.49) | data formatting | bytes 3145728 | tf_op jit(solution)/shard_map/all_to_all | solution.py:62
  291.1 9.5 %reshape.168 = bf16[8,2,49152]{2,1,0:T(2,128)(2,1)} reshape(bf16[12288,1,2,32]{3,2,1,0:T(2,128)(2,1)} %bitcast.74) | data formatting | bytes 3145728
  300.6 4.8 %all-to-all-start.4 = ((bf16[8,2,49152]{2,1,0:T(2,128)(2,1)}), bf16[8,2,49152]{2,1,0:T(2,128)(2,1)S(1)}, u32[]{:S(2)}, u32[]{:S(2)}) async-start(bf16[8,2,49152]{2,1,0:T(2,128)(2,1)} %reshape.168), calls=%async_computation.4 | async-start | bytes 3145728 | tf_op jit(solution)/shard_map/all_to_all | solution.py:63
  305.4 24.0 %all-to-all-done.4 = bf16[8,2,49152]{2,1,0:T(2,128)(2,1)S(1)} async-done(((bf16[8,2,49152]{2,1,0:T(2,128)(2,1)}), bf16[8,2,49152]{2,1,0:T(2,128)(2,1)S(1)}, u32[]{:S(2)}, u32[]{:S(2)}) %all-to-all-start.4) | async-done | bytes 1572896 | tf_op jit(solution)/shard_map/all_to_all | solution.py:63
  329.4 5.4 %reshape.169 = bf16[12288,1,2,32]{3,2,1,0:T(2,128)(2,1)} reshape(bf16[8,2,49152]{2,1,0:T(2,128)(2,1)S(1)} %all-to-all-done.4) | data formatting | bytes 3145728
  334.9 14.4 %copy.75 = bf16[32,1,2,8,1536]{4,2,3,0,1:T(2,128)(2,1)S(1)} copy(bf16[32,1,2,8,1536]{0,2,4,3,1:T(2,128)(2,1)} %bitcast.75) | data formatting | bytes 3145728 | tf_op jit(solution)/shard_map/all_to_all | solution.py:63
  357.0 8.8 %copy.77 = f32[512,32,48]{2,1,0:T(8,128)} copy(f32[512,32,48]{0,2,1:T(8,128)} %bitcast.76) | data formatting | bytes 6291456 | tf_op jit(solution)/shard_map/convert_element_type | solution.py:66
  365.8 6.5 %fusion.2 = bf16[32,48,512]{1,0,2:T(8,128)(2,1)} fusion(f32[512,32,48]{2,1,0:T(8,128)} %copy.77, f32[48,512]{0,1:T(8,128)S(1)} %broadcast_multiply_fusion), kind=kLoop, calls=%fused_computation.10 | loop fusion | flops 1572864 | bytes 4816896 | tf_op jit(solution)/shard_map/convert_element_type | solution.py:66
  372.3 5.4 %copy.78 = bf16[32,48,512]{2,1,0:T(8,128)(2,1)} copy(bf16[32,48,512]{1,0,2:T(8,128)(2,1)} %fusion.2) | data formatting | bytes 3145728
  (61 shorter events, 41.7 us)
Async XLA Ops:
  7.2 16.2 %copy-start = (f32[32,128]{1,0:T(8,128)S(1)}, f32[32,128]{1,0:T(8,128)}, u32[]{:S(2)}) copy-start(f32[32,128]{1,0:T(8,128)} %param.9) | copy-start | bytes 49156
  7.2 103.9 %all-reduce.2.cloned.1.call-start = ((), (), s32[]{:S(2)}) async-start(), calls=%async_computation.5 | async-start | bytes 524288 | tf_op jit(solution)/shard_map/psum | solution.py:32
  14.5 4.8 %copy-start.4 = (s32[512]{0:T(512)S(1)}, s32[512]{0:T(512)}, u32[]{:S(2)}) copy-start(s32[512]{0:T(512)} %param.11) | copy-start | bytes 6148
  130.6 21.1 %all-to-all-start.1 = ((bf16[32,8,2,1536]{3,2,0,1:T(2,128)(2,1)}), bf16[32,8,2,1536]{3,2,0,1:T(2,128)(2,1)S(1)}, u32[]{:S(2)}, u32[]{:S(2)}) async-start(bf16[32,8,2,1536]{3,2,0,1:T(2,128)(2,1)} %copy.65), calls=%async_computation.1 | async-start | bytes 3145728 | tf_op jit(solution)/shard_map/all_to_all | solution.py:46
  151.6 14.2 %all-to-all-start = ((s32[32,1,2]{2,1,0:T(1,128)}), s32[32,1,2]{2,1,0:T(1,128)S(1)}, u32[]{:S(2)}, u32[]{:S(2)}) async-start(s32[32,1,2]{2,1,0:T(1,128)} %constant_dynamic-slice_fusion), calls=%async_computation | async-start | bytes 32768 | tf_op jit(solution)/shard_map/all_to_all | solution.py:29
  165.8 43.8 %all-to-all-start.2 = ((bf16[32,1,2,12288]{3,2,1,0:T(2,128)(2,1)}), bf16[32,1,2,12288]{3,2,1,0:T(2,128)(2,1)S(1)}, u32[]{:S(2)}, u32[]{:S(2)}) async-start(bf16[32,1,2,12288]{3,2,1,0:T(2,128)(2,1)} %reshape.160), calls=%async_computation.2 | async-start | bytes 3145728 | tf_op jit(solution)/shard_map/all_to_all | solution.py:45
  171.8 43.0 %copy-start.3 = (bf16[4,256,256]{2,1,0:T(8,128)(2,1)S(1)}, bf16[4,256,256]{2,1,0:T(8,128)(2,1)}, u32[]{:S(2)}) copy-start(bf16[4,256,256]{2,1,0:T(8,128)(2,1)} %param.10) | copy-start | bytes 1572868
  214.8 3.6 copy-start.2
  300.6 4.8 %copy-start.6 = (s32[128]{0:T(128)S(1)}, s32[128]{0:T(128)}, u32[]{:S(2)}) copy-start(s32[128]{0:T(128)} %param.13) | copy-start | bytes 1540
  300.6 28.8 %all-to-all-start.4 = ((bf16[8,2,49152]{2,1,0:T(2,128)(2,1)}), bf16[8,2,49152]{2,1,0:T(2,128)(2,1)S(1)}, u32[]{:S(2)}, u32[]{:S(2)}) async-start(bf16[8,2,49152]{2,1,0:T(2,128)(2,1)} %reshape.168), calls=%async_computation.4 | async-start | bytes 3145728 | tf_op jit(solution)/shard_map/all_to_all | solution.py:63
  372.3 8.5 %copy-start.5 = (f32[48]{0:T(128)S(1)}, f32[48]{0:T(128)}, u32[]{:S(2)}) copy-start(f32[48]{0:T(128)} %param.12) | copy-start | bytes 580
  372.3 10.1 %copy-start.1 = (f32[32,128]{1,0:T(8,128)S(1)}, f32[32,128]{1,0:T(8,128)}, u32[]{:S(2)}) copy-start(f32[32,128]{1,0:T(8,128)} %param.9) | copy-start | bytes 49156
Sparse Core Ops, SparseCore 0:
  19.4 91.6 all-reduce.1
where the time goes:
time: 391 us; the launch traced here: 389 us
  waiting for transfers between devices  165 us (42%)
  local copies, waits for them, and re-layouts  110 us (28%)
  blocking collectives  44.2 us (11%)
  other arithmetic  23.1 us (6%)
  starting transfers between devices  22.4 us (6%)
  between operations  14.4 us (4%)
  matrix products  10.2 us (3%)
    psum x1, waiting for transfers between devices, local(): summed = lax.psum(jnp.sum(ensemble, axis=0, dtype=jnp.float32), 'member')  83.8 us
    all_to_all x1, blocking collectives, local(): lax.all_to_all(result_rows, 'space', split_axis=0, concat_axis=0, tiled=T...  44.2 us
    all_to_all x1, waiting for transfers between devices, local(): lax.all_to_all(lax.all_to_all(payload, 'member', split_axis=1, concat_axi...  37.2 us
    unnamed x18, local copies, waits for them, and re-layouts  27.6 us
    all_to_all x1, waiting for transfers between devices, local(): lax.all_to_all(halfway, 'member', split_axis=3, concat_axis=1, tiled=True)  24 us
    all_to_all x1, waiting for transfers between devices, local(): lax.all_to_all(payload, 'member', split_axis=1, concat_axis=3, tiled=True)  16.7 us
    all_to_all x1, local copies, waits for them, and re-layouts, local(): lax.all_to_all(halfway, 'member', split_axis=3, concat_axis=1, tiled=True)  14.4 us
    convert_element_type x2, local copies, waits for them, and re-layouts, local(): analysis = (mean[None] + restored.astype(jnp.float32)).astype(jnp.bfloat16)  11.2 us
  transfers between devices with their start and end apart: 5, of which 5 were waited for; matrix products, arithmetic and copies ran while one was open for 3% of the time, Pallas kernels for 0%

commit v1 on v0

--- a/solution.py
+++ b/solution.py
@@ -29,7 +29,7 @@
     got_labels = lax.all_to_all(
         my_labels, "space", split_axis=0, concat_axis=0, tiled=True
     ).reshape(own_cols)
-    summed = lax.psum(jnp.sum(ensemble, axis=0, dtype=jnp.float32), "member")
+    summed = jnp.sum(lax.all_gather(jnp.sum(ensemble, axis=0, dtype=jnp.float32), "member"), axis=0)
     mean = summed / members
     region_hot = (jnp.arange(all_regions, dtype=jnp.int32)[:, None] == region_ids[None, :]).astype(
         jnp.float32

time: 391 us -> 331 us (0.85)
  waiting for transfers between devices: 165 us -> 78.9 us
  blocking collectives: 44.2 us -> 79.7 us
  between operations: 14.4 us -> 0.98 us
  starting transfers between devices: 22.4 us -> 27.9 us
    psum x1 -> x0, waiting for transfers between devices: 83.8 us -> none  [local(): summed = lax.psum(jnp.sum(ensemble, axis=0, dtype=jnp.float32), 'member')]
    all_gather x0 -> x1, blocking collectives: none -> 35.4 us  [local(): lax.all_gather(jnp.sum(ensemble, axis=0, dtype=jnp.float32), 'member')]
    unnamed x18 -> x20, local copies, waits for them, and re-layouts: 27.6 us -> 26.9 us
  transfers between devices with their start and end apart: 5 -> 4, of which waited for: 5 -> 4; matrix products, arithmetic and copies ran while one was open for 3% -> 1% of each run, Pallas kernels for 0% -> 0%
where the time goes in v1:
time: 331 us; the launch traced here: 330 us
  local copies, waits for them, and re-layouts  110 us (33%)
  blocking collectives  79.7 us (24%)
  waiting for transfers between devices  78.9 us (24%)
  starting transfers between devices  27.9 us (8%)
  other arithmetic  22.3 us (7%)
  matrix products  10.2 us (3%)
    all_to_all x1, blocking collectives, local(): lax.all_to_all(result_rows, 'space', split_axis=0, concat_axis=0, tiled=T...  44.2 us
    all_to_all x1, waiting for transfers between devices, local(): lax.all_to_all(lax.all_to_all(payload, 'member', split_axis=1, concat_axi...  37.2 us
    all_gather x1, blocking collectives, local(): lax.all_gather(jnp.sum(ensemble, axis=0, dtype=jnp.float32), 'member')  35.4 us
    unnamed x20, local copies, waits for them, and re-layouts  26.9 us
    all_to_all x1, waiting for transfers between devices, local(): lax.all_to_all(halfway, 'member', split_axis=3, concat_axis=1, tiled=True)  24 us
    all_to_all x1, waiting for transfers between devices, local(): lax.all_to_all(payload, 'member', split_axis=1, concat_axis=3, tiled=True)  14.9 us
    all_to_all x1, local copies, waits for them, and re-layouts, local(): lax.all_to_all(halfway, 'member', split_axis=3, concat_axis=1, tiled=True)  14.4 us
    convert_element_type x2, local copies, waits for them, and re-layouts, local(): analysis = (mean[None] + restored.astype(jnp.float32)).astype(jnp.bfloat16)  11.2 us
  transfers between devices with their start and end apart: 4, of which 4 were waited for; matrix products, arithmetic and copies ran while one was open for 1% of the time, Pallas kernels for 0%

profile of v1, /device:TPU:64, one launch (start us, length us, event | category | flops | bytes accessed | tf_op | source)
XLA Modules:
  0.0 329.9 jit_solution(7407053213847845103)
XLA Ops:
  5.5 3.5 %gather_fusion = s32[512]{0:T(512)S(1)} fusion(s32[512]{0:T(512)S(1)} %get-tuple-element.21, s32[1024]{0:T(1024)S(1)} %pad_clamp_fusion.2), kind=kCustom, calls=%fused_computation.2 | custom fusion | bytes 6144 | tf_op jit(solution)/shard_map/jit(_take)/gather | solution.py:27
  9.0 6.5 %copy.61 = bf16[32,48,512]{1,0,2:T(8,128)(2,1)} copy(bf16[32,48,512]{2,1,0:T(8,128)(2,1)S(1)} %copy-done.3) | data formatting | bytes 3145728 | tf_op args[0]
  15.6 4.1 %convert_reduce_fusion = f32[48,512]{0,1:T(8,128)S(1)} fusion(bf16[32,48,512]{1,0,2:T(8,128)(2,1)} %copy.61), kind=kLoop, calls=%fused_computation.6 | loop fusion | flops 1548288 | bytes 1671168 | tf_op jit(solution)/shard_map/reduce_sum | solution.py:32
  19.7 35.4 %all-gather = f32[384,512]{1,0:T(8,128)S(1)} all-gather(f32[48,512]{1,0:T(8,128)S(1)} %copy.62), channel_id=2, replica_groups=mesh['member'=8,'space'=32] {'member'}, dimensions={0}, use_global_device_ids=true | all-gather | bytes 884736 | tf_op jit(solution)/shard_map/all_gather | solution.py:32
  55.8 5.8 %fusion.3 = bf16[512,32,48]{2,1,0:T(8,128)(2,1)} fusion(bf16[32,48,512]{1,0,2:T(8,128)(2,1)} %copy.61, f32[32,512]{0,1:T(8,128)S(1)} %copy.65, f32[48,512]{0,1:T(8,128)S(1)} %copy.63), kind=kLoop, calls=%fused_computation.11 | loop fusion | flops 3145728 | bytes 3309568 | tf_op jit(solution)/shard_map/transpose | solution.py:41
  61.6 4.4 %copy.66 = bf16[512,32,48]{0,2,1:T(8,128)(2,1)S(1)} copy(bf16[512,32,48]{2,1,0:T(8,128)(2,1)} %fusion.3) | data formatting | bytes 3145728 | tf_op jit(solution)/shard_map/transpose | solution.py:41
  74.3 7.0 %all-to-all-start.1 = ((bf16[32,8,2,1536]{3,2,0,1:T(2,128)(2,1)}), bf16[32,8,2,1536]{3,2,0,1:T(2,128)(2,1)S(1)}, u32[]{:S(2)}, u32[]{:S(2)}) async-start(bf16[32,8,2,1536]{3,2,0,1:T(2,128)(2,1)} %copy.68), calls=%async_computation.1 | async-start | bytes 3145728 | tf_op jit(solution)/shard_map/all_to_all | solution.py:46
  82.0 14.9 %all-to-all-done.1 = bf16[32,8,2,1536]{3,2,0,1:T(2,128)(2,1)S(1)} async-done(((bf16[32,8,2,1536]{3,2,0,1:T(2,128)(2,1)}), bf16[32,8,2,1536]{3,2,0,1:T(2,128)(2,1)S(1)}, u32[]{:S(2)}, u32[]{:S(2)}) %all-to-all-start.1) | async-done | bytes 1572896 | tf_op jit(solution)/shard_map/all_to_all | solution.py:46
  96.9 8.8 %all-to-all-start = ((s32[32,1,2]{2,1,0:T(1,128)}), s32[32,1,2]{2,1,0:T(1,128)S(1)}, u32[]{:S(2)}, u32[]{:S(2)}) async-start(s32[32,1,2]{2,1,0:T(1,128)} %constant_dynamic-slice_fusion), calls=%async_computation | async-start | bytes 32768 | tf_op jit(solution)/shard_map/all_to_all | solution.py:29
  112.0 6.0 %all-to-all-start.2 = ((bf16[32,1,2,12288]{3,2,1,0:T(2,128)(2,1)}), bf16[32,1,2,12288]{3,2,1,0:T(2,128)(2,1)S(1)}, u32[]{:S(2)}, u32[]{:S(2)}) async-start(bf16[32,1,2,12288]{3,2,1,0:T(2,128)(2,1)} %reshape.163), calls=%async_computation.2 | async-start | bytes 3145728 | tf_op jit(solution)/shard_map/all_to_all | solution.py:45
  118.7 37.2 %all-to-all-done.2 = bf16[32,1,2,12288]{3,2,1,0:T(2,128)(2,1)S(1)} async-done(((bf16[32,1,2,12288]{3,2,1,0:T(2,128)(2,1)}), bf16[32,1,2,12288]{3,2,1,0:T(2,128)(2,1)S(1)}, u32[]{:S(2)}, u32[]{:S(2)}) %all-to-all-start.2) | async-done | bytes 1572896 | tf_op jit(solution)/shard_map/all_to_all | solution.py:45
  155.8 5.2 %reshape.103 = bf16[64,256,48]{2,1,0:T(8,128)(2,1)} reshape(bf16[32,1,2,12288]{3,2,1,0:T(2,128)(2,1)S(1)} %all-to-all-done.2) | data formatting | bytes 3145728 | tf_op jit(solution)/shard_map/reshape | solution.py:52
  161.0 3.6 %fusion.10 = f32[64,48,256]{2,1,0:T(8,128)S(1)} fusion(bf16[64,256,48]{2,1,0:T(8,128)(2,1)} %reshape.103, bf16[4,256,256]{2,1,0:T(8,128)(2,1)S(1)} %copy-done.4), kind=kOutput, calls=%fused_computation.24 | convolution fusion | flops 402653184 | bytes 4849664 | tf_op jit(solution)/shard_map/jk,cjt->ckt/dot_general | solution.py:55
  172.6 9.3 %reshape.104 = bf16[32,1,2,12288]{3,2,0,1:T(2,128)(2,1)S(1)} reshape(bf16[64,256,48]{2,1,0:T(8,128)(2,1)} %copy.75) | data formatting | bytes 3145728 | tf_op jit(solution)/shard_map/reshape | solution.py:61
  181.9 44.2 %all_to_all.49 = bf16[32,1,2,12288]{3,2,1,0:T(2,128)(2,1)S(1)} all-to-all(bf16[32,1,2,12288]{3,2,1,0:T(2,128)(2,1)S(1)} %bitcast.80), channel_id=1, replica_groups=mesh['member'=8,'space'=32] {'space'}, dimensions={0} | all-to-all | bytes 3145728 | tf_op jit(solution)/shard_map/all_to_all | solution.py:62
  226.1 11.1 %copy.77 = bf16[32,1,2,12288]{0,2,1,3:T(2,128)(2,1)} copy(bf16[32,1,2,12288]{3,2,1,0:T(2,128)(2,1)S(1)} %all_to_all.49) | data formatting | bytes 3145728 | tf_op jit(solution)/shard_map/all_to_all | solution.py:62
  237.2 9.5 %reshape.171 = bf16[8,2,49152]{2,1,0:T(2,128)(2,1)} reshape(bf16[12288,1,2,32]{3,2,1,0:T(2,128)(2,1)} %bitcast.75) | data formatting | bytes 3145728
  246.7 6.1 %all-to-all-start.4 = ((bf16[8,2,49152]{2,1,0:T(2,128)(2,1)}), bf16[8,2,49152]{2,1,0:T(2,128)(2,1)S(1)}, u32[]{:S(2)}, u32[]{:S(2)}) async-start(bf16[8,2,49152]{2,1,0:T(2,128)(2,1)} %reshape.171), calls=%async_computation.4 | async-start | bytes 3145728 | tf_op jit(solution)/shard_map/all_to_all | solution.py:63
  252.9 24.0 %all-to-all-done.4 = bf16[8,2,49152]{2,1,0:T(2,128)(2,1)S(1)} async-done(((bf16[8,2,49152]{2,1,0:T(2,128)(2,1)}), bf16[8,2,49152]{2,1,0:T(2,128)(2,1)S(1)}, u32[]{:S(2)}, u32[]{:S(2)}) %all-to-all-start.4) | async-done | bytes 1572896 | tf_op jit(solution)/shard_map/all_to_all | solution.py:63
  276.9 5.4 %reshape.172 = bf16[12288,1,2,32]{3,2,1,0:T(2,128)(2,1)} reshape(bf16[8,2,49152]{2,1,0:T(2,128)(2,1)S(1)} %all-to-all-done.4) | data formatting | bytes 3145728
  282.3 14.4 %copy.78 = bf16[32,1,2,8,1536]{4,2,3,0,1:T(2,128)(2,1)S(1)} copy(bf16[32,1,2,8,1536]{0,2,4,3,1:T(2,128)(2,1)} %bitcast.76) | data formatting | bytes 3145728 | tf_op jit(solution)/shard_map/all_to_all | solution.py:63
  304.5 8.8 %copy.80 = f32[512,32,48]{2,1,0:T(8,128)} copy(f32[512,32,48]{0,2,1:T(8,128)} %bitcast.77) | data formatting | bytes 6291456 | tf_op jit(solution)/shard_map/convert_element_type | solution.py:66
  313.2 6.5 %fusion.2 = bf16[32,48,512]{1,0,2:T(8,128)(2,1)} fusion(f32[512,32,48]{2,1,0:T(8,128)} %copy.80, f32[48,512]{0,1:T(8,128)S(1)} %copy.63), kind=kLoop, calls=%fused_computation.10 | loop fusion | flops 1572864 | bytes 4816896 | tf_op jit(solution)/shard_map/convert_element_type | solution.py:66
  319.8 5.4 %copy.81 = bf16[32,48,512]{2,1,0:T(8,128)(2,1)} copy(bf16[32,48,512]{1,0,2:T(8,128)(2,1)} %fusion.2) | data formatting | bytes 3145728
  (64 shorter events, 41.8 us)
Async XLA Ops:
  0.6 54.8 %copy-start = (f32[32,128]{1,0:T(8,128)S(1)}, f32[32,128]{1,0:T(8,128)}, u32[]{:S(2)}) copy-start(f32[32,128]{1,0:T(8,128)} %param.9) | copy-start | bytes 49156
  0.6 8.4 %copy-start.3 = (bf16[32,48,512]{2,1,0:T(8,128)(2,1)S(1)}, bf16[32,48,512]{2,1,0:T(8,128)(2,1)}, u32[]{:S(2)}) copy-start(bf16[32,48,512]{2,1,0:T(8,128)(2,1)} %param.8) | copy-start | bytes 4718596
  15.6 39.8 %copy-start.5 = (s32[512]{0:T(512)S(1)}, s32[512]{0:T(512)}, u32[]{:S(2)}) copy-start(s32[512]{0:T(512)} %param.11) | copy-start | bytes 6148
  74.3 22.6 %all-to-all-start.1 = ((bf16[32,8,2,1536]{3,2,0,1:T(2,128)(2,1)}), bf16[32,8,2,1536]{3,2,0,1:T(2,128)(2,1)S(1)}, u32[]{:S(2)}, u32[]{:S(2)}) async-start(bf16[32,8,2,1536]{3,2,0,1:T(2,128)(2,1)} %copy.68), calls=%async_computation.1 | async-start | bytes 3145728 | tf_op jit(solution)/shard_map/all_to_all | solution.py:46
  96.9 15.0 %all-to-all-start = ((s32[32,1,2]{2,1,0:T(1,128)}), s32[32,1,2]{2,1,0:T(1,128)S(1)}, u32[]{:S(2)}, u32[]{:S(2)}) async-start(s32[32,1,2]{2,1,0:T(1,128)} %constant_dynamic-slice_fusion), calls=%async_computation | async-start | bytes 32768 | tf_op jit(solution)/shard_map/all_to_all | solution.py:29
  112.0 43.8 %all-to-all-start.2 = ((bf16[32,1,2,12288]{3,2,1,0:T(2,128)(2,1)}), bf16[32,1,2,12288]{3,2,1,0:T(2,128)(2,1)S(1)}, u32[]{:S(2)}, u32[]{:S(2)}) async-start(bf16[32,1,2,12288]{3,2,1,0:T(2,128)(2,1)} %reshape.163), calls=%async_computation.2 | async-start | bytes 3145728 | tf_op jit(solution)/shard_map/all_to_all | solution.py:45
  118.0 43.0 %copy-start.4 = (bf16[4,256,256]{2,1,0:T(8,128)(2,1)S(1)}, bf16[4,256,256]{2,1,0:T(8,128)(2,1)}, u32[]{:S(2)}) copy-start(bf16[4,256,256]{2,1,0:T(8,128)(2,1)} %param.10) | copy-start | bytes 1572868
  161.0 3.6 %copy-start.2 = (bf16[64,256,48]{2,1,0:T(8,128)(2,1)S(1)}, bf16[64,256,48]{2,1,0:T(8,128)(2,1)}, u32[]{:S(2)}) copy-start(bf16[64,256,48]{2,1,0:T(8,128)(2,1)} %reshape.103) | copy-start | bytes 4718596
  246.7 6.1 %copy-start.7 = (s32[128]{0:T(128)S(1)}, s32[128]{0:T(128)}, u32[]{:S(2)}) copy-start(s32[128]{0:T(128)} %param.13) | copy-start | bytes 1540
  246.7 30.1 %all-to-all-start.4 = ((bf16[8,2,49152]{2,1,0:T(2,128)(2,1)}), bf16[8,2,49152]{2,1,0:T(2,128)(2,1)S(1)}, u32[]{:S(2)}, u32[]{:S(2)}) async-start(bf16[8,2,49152]{2,1,0:T(2,128)(2,1)} %reshape.171), calls=%async_computation.4 | async-start | bytes 3145728 | tf_op jit(solution)/shard_map/all_to_all | solution.py:63
  319.8 8.5 %copy-start.6 = (f32[48]{0:T(128)S(1)}, f32[48]{0:T(128)}, u32[]{:S(2)}) copy-start(f32[48]{0:T(128)} %param.12) | copy-start | bytes 580
  319.8 10.1 %copy-start.1 = (f32[32,128]{1,0:T(8,128)S(1)}, f32[32,128]{1,0:T(8,128)}, u32[]{:S(2)}) copy-start(f32[32,128]{1,0:T(8,128)} %param.9) | copy-start | bytes 49156
